TPU v7x, 256 devices: a whole 4x4x8 slice. The times are simulated.
256 devices in a mesh: row: 8 (over z_hi, x), col: 32 (over z_lo, y, core).
Axes of the slice: x: 4, y: 4, z: 8 (z_hi: 2, z_lo: 4; z = z_hi * 4 + z_lo), core: 2. Of those that a mesh axis runs over, the one named last changes fastest.
Arguments:
- region_factors: bfloat16 [262144, 512], P(('row', 'col')), may hold values from -1.25 to 1.25
- item_factors: bfloat16 [32, 128, 512], P('col', 'row'), may hold values from -1.25 to 1.25
- slab_blocks: bfloat16 [256, 32, 6, 128, 128], P(('row', 'col')), may hold values from -6 to 6
- block_rows: int32 [256, 32, 6], P(('row', 'col')), may hold values from 0 to 7, as said below
- counts: int32 [256, 32], P(('row', 'col')), may hold values from 1 to 6, as said below
Outputs:
- new_regions: float32 [262144, 512], P(('row', 'col'))
- new_items: float32 [32, 128, 512], P('col', 'row')
Inputs may be any that keep to these rules, and one draw needn't show every extreme that they name: `counts`: every entry is at least 1; some device-block has exactly 6 present blocks in some block column. `block_rows`: for each device-block and block column, the first counts[d, p] entries are distinct; entries at slots s >= counts[d, p] (and their slab blocks) are not used.
All inputs are finite; a program needn't handle non-finite values.
Results may differ from a plain program's by a relative error of at most 0.0023.
Values may be sent and summed in bfloat16 or wider, within the bound.
No kernel may reach another device: no remote copies, remote signals or barrier semaphores. Data moves between devices by JAX's collectives and lax.ppermute only.
A program may use at most 128 MiB of HBM per device.

v0:
```python
import jax
import jax.numpy as jnp
from jax import lax
from jax.sharding import PartitionSpec as P

region_rate = 0.05
item_rate = 0.01
decay_rate = 0.1


def passed_along(value, axis, steps):
    count = lax.axis_size(axis)
    pairs = [(source, (source + steps) % count) for source in range(count)]
    return lax.ppermute(value, axis, pairs)


def pass_panel(panel_now):
    return passed_along(panel_now, "col", 1)


def on_device(region_factors, item_factors, slab_blocks, block_rows, counts):
    cycle_size = lax.axis_size("col")
    position = lax.axis_index("col")
    block_size = slab_blocks.shape[-1]
    factor_width = region_factors.shape[-1]
    slot_total = slab_blocks.shape[2]
    row_blocks = region_factors.shape[0] // block_size
    region_blocks = region_factors.reshape(row_blocks, block_size, factor_width)
    tiles_all = slab_blocks[0]
    row_lists = block_rows[0]
    live_counts = counts[0]
    slot_ids = jnp.arange(slot_total, dtype=jnp.int32)
    panel_start = lax.all_gather(item_factors, "row", axis=1, tiled=True)[0]
    region_zero = jnp.zeros((row_blocks, block_size, factor_width), jnp.float32)
    item_zero = jnp.zeros((block_size, factor_width), jnp.float32)

    def padded_work(column, panel_now, region_totals):
        rows_now = lax.dynamic_index_in_dim(row_lists, column, 0, keepdims=False)
        tiles_now = lax.dynamic_index_in_dim(tiles_all, column, 0, keepdims=False)
        count_now = lax.dynamic_index_in_dim(live_counts, column, 0, keepdims=False)
        chosen = jnp.take(region_blocks, rows_now, axis=0)
        predicted = jnp.einsum("sik,jk->sij", chosen, panel_now, preferred_element_type=jnp.float32)
        present = slot_ids < count_now
        residual = jnp.where(present[:, None, None], predicted - tiles_now.astype(jnp.float32), 0.0)
        residual = residual.astype(jnp.bfloat16)
        update = jnp.einsum("sij,jk->sik", residual, panel_now, preferred_element_type=jnp.float32)
        region_totals = region_totals.at[rows_now].add(update)
        item_part = jnp.einsum("sij,sik->jk", residual, chosen, preferred_element_type=jnp.float32)
        return (region_totals, item_part)

    def block_work(column, panel_now, region_totals):
        return padded_work(column, panel_now, region_totals)

    last_column = (position + 1) % cycle_size

    def cycle_travel(passed, carried):
        panel_now, grad_now, region_totals = carried
        column = (position - passed) % cycle_size
        region_totals, item_part = block_work(column, panel_now, region_totals)
        grad_now = grad_now + item_part
        panel_now = pass_panel(panel_now)
        grad_now = passed_along(grad_now, "col", 1)
        return (panel_now, grad_now, region_totals)

    panel_now, grad_now, region_totals = lax.fori_loop(
        0, cycle_size - 1, cycle_travel, (panel_start, item_zero, region_zero)
    )
    region_totals, item_part = block_work(last_column, panel_now, region_totals)
    grad_home = passed_along(grad_now + item_part, "col", 1)
    own_piece = lax.psum_scatter(grad_home, "row", scatter_dimension=0, tiled=True)
    regions_wide = region_factors.astype(jnp.float32)
    region_grad = region_totals.reshape(row_blocks * block_size, factor_width)
    new_regions = regions_wide - region_rate * (region_grad + decay_rate * regions_wide)
    own_rows = item_factors[0].astype(jnp.float32)
    new_items = (own_rows - item_rate * (own_piece + decay_rate * own_rows))[None]
    return (new_regions, new_items)


def solution(mesh):
    return jax.shard_map(
        on_device,
        mesh=mesh,
        in_specs=(
            P(("row", "col"), None),
            P("col", "row", None),
            P(("row", "col"), None, None, None, None),
            P(("row", "col"), None, None),
            P(("row", "col"), None),
        ),
        out_specs=(P(("row", "col"), None), P("col", "row", None)),
        check_vma=False,
    )
```

profile of v0, /device:TPU:8, one launch (start us, length us, event | category | flops | bytes accessed | tf_op | source)
XLA Modules:
  0.0 607.2 jit_solution(15959370318166916743)
XLA Ops:
  11.0 46.2 %all_gather.3 = bf16[1,128,512]{2,1,0:T(8,128)(2,1)S(1)} all-gather(bf16[1,16,512]{2,1,0:T(8,128)(2,1)} %param.10), channel_id=1, replica_groups=mesh['row'=8,'col'=32] {'row'}, dimensions={1}, use_global_device_ids=true | all-gather | bytes 147456 | tf_op jit(solution)/shard_map/all_gather | solution.py:33
  57.1 2.7 gather_fusion.1
  61.5 430.5 %while.20 = (s32[]{:T(128)}, bf16[128,512]{1,0:T(8,128)(2,1)S(1)}, f32[128,512]{1,0:T(8,128)S(1)}, f32[8,128,512]{2,1,0:T(8,128)}, s32[]{:T(128)}, /*index=5*/s3...) while((s32[]{:T(128)}, bf16[128,512]{1,0:T(8,128)(2,1)S(1)}, ...), condition=%wide.region_2.4_spmd.clone, body=%wide.region_0.3_spmd.clone.sunk | while | flops 303629376 | bytes 12849738 | solution.py:65
  67.9 3.9 scatter_fusion
  78.3 3.9 scatter_fusion
  88.8 3.9 scatter_fusion
  99.9 3.9 scatter_fusion
  112.5 3.9 scatter_fusion
  116.4 3.0 collective-permute-done.1
  125.0 4.0 scatter_fusion
  129.0 4.7 collective-permute-done.1
  138.5 3.9 scatter_fusion
  142.4 5.7 collective-permute-done.1
  152.8 3.9 scatter_fusion
  156.7 5.7 collective-permute-done.1
  167.2 3.9 scatter_fusion
  171.1 5.7 collective-permute-done.1
  181.5 4.0 scatter_fusion
  185.5 5.5 collective-permute-done.1
  195.8 3.9 scatter_fusion
  199.7 5.7 collective-permute-done.1
  210.2 3.9 scatter_fusion
  214.1 5.7 collective-permute-done.1
  224.5 3.9 scatter_fusion
  228.4 5.7 collective-permute-done.1
  238.8 3.9 scatter_fusion
  242.7 5.7 collective-permute-done.1
  253.2 3.9 scatter_fusion
  257.1 5.6 collective-permute-done.1
  267.5 3.9 scatter_fusion
  271.4 5.7 collective-permute-done.1
  281.8 3.9 scatter_fusion
  285.7 5.7 collective-permute-done.1
  296.2 3.9 scatter_fusion
  300.1 5.7 collective-permute-done.1
  310.5 3.9 scatter_fusion
  314.4 5.7 collective-permute-done.1
  324.8 3.9 scatter_fusion
  328.7 5.7 collective-permute-done.1
  339.2 3.9 scatter_fusion
  343.1 5.7 collective-permute-done.1
  353.5 3.9 scatter_fusion
  357.4 5.7 collective-permute-done.1
  367.8 3.9 scatter_fusion
  371.7 5.7 collective-permute-done.1
  382.2 3.9 scatter_fusion
  386.1 5.7 collective-permute-done.1
  396.5 3.9 scatter_fusion
  400.4 5.7 collective-permute-done.1
  410.8 3.9 scatter_fusion
  414.7 5.7 collective-permute-done.1
  425.2 3.9 scatter_fusion
  429.1 5.7 collective-permute-done.1
  439.5 3.9 scatter_fusion
  443.4 5.7 collective-permute-done.1
  453.8 3.9 scatter_fusion
  457.7 5.7 collective-permute-done.1
  468.2 3.9 scatter_fusion
  472.1 5.6 collective-permute-done.1
  482.5 3.9 scatter_fusion
  486.4 5.7 collective-permute-done.1
  495.7 8.2 %collective-permute-done.2 = f32[128,512]{1,0:T(8,128)S(1)} collective-permute-done((f32[128,512]{1,0:T(8,128)S(1)}, f32[128,512]{1,0:T(8,128)S(1)}, u32[]{:S(2)}, u32[]{:S(2)}) %collective-permute-start.2) | collective-permute-done | bytes 262176 | tf_op jit(solution)/shard_map/ppermute | solution.py:14
  504.6 2.9 scatter_fusion.1
  509.2 89.8 %reduce-scatter.2.cloned.1.call-done = f32[16,512]{1,0:T(8,128)} async-done(((f32[128,512]{1,0:T(8,128)}), f32[16,512]{1,0:T(8,128)}) %reduce-scatter.2.cloned.1.call-update) | async-done | bytes 32784 | tf_op jit(solution)/shard_map/reduce_scatter | solution.py:70
  (436 shorter events, 170.8 us)
Async XLA Ops:
  7.2 591.8 %reduce-scatter.2.cloned.1.call-start = ((), (), s32[]{:S(2)}) async-start(), calls=%async_computation.1 | async-start | bytes 294912 | tf_op jit(solution)/shard_map/reduce_scatter | solution.py:70
  61.5 10.3 %collective-permute-start = (bf16[128,512]{1,0:T(8,128)(2,1)S(1)}, bf16[128,512]{1,0:T(8,128)(2,1)S(1)}, u32[]{:S(2)}, u32[]{:S(2)}) collective-permute-start(bf16[128,512]{1,0:T(8,128)(2,1)S(1)} %copy.21), channel_id=1, source_target_pairs={{0,1},{1,2},{2,3},{3,4},{4,5},{5,6},{6,7},{7,8},{8,9},{9,10},{10,1... | collective-permute-start | bytes 393224 | tf_op jit(solution)/shard_map/while/body/eval_jaxpr/ppermute | solution.py:14
  65.9 6.0 collective-permute-start.1
  71.9 10.3 %collective-permute-start = (bf16[128,512]{1,0:T(8,128)(2,1)S(1)}, bf16[128,512]{1,0:T(8,128)(2,1)S(1)}, u32[]{:S(2)}, u32[]{:S(2)}) collective-permute-start(bf16[128,512]{1,0:T(8,128)(2,1)S(1)} %copy.21), channel_id=1, source_target_pairs={{0,1},{1,2},{2,3},{3,4},{4,5},{5,6},{6,7},{7,8},{8,9},{9,10},{10,1... | collective-permute-start | bytes 393224 | tf_op jit(solution)/shard_map/while/body/eval_jaxpr/ppermute | solution.py:14
  76.3 6.0 collective-permute-start.1
  82.4 10.3 %collective-permute-start = (bf16[128,512]{1,0:T(8,128)(2,1)S(1)}, bf16[128,512]{1,0:T(8,128)(2,1)S(1)}, u32[]{:S(2)}, u32[]{:S(2)}) collective-permute-start(bf16[128,512]{1,0:T(8,128)(2,1)S(1)} %copy.21), channel_id=1, source_target_pairs={{0,1},{1,2},{2,3},{3,4},{4,5},{5,6},{6,7},{7,8},{8,9},{9,10},{10,1... | collective-permute-start | bytes 393224 | tf_op jit(solution)/shard_map/while/body/eval_jaxpr/ppermute | solution.py:14
  86.8 6.0 collective-permute-start.1
  92.8 11.1 %collective-permute-start = (bf16[128,512]{1,0:T(8,128)(2,1)S(1)}, bf16[128,512]{1,0:T(8,128)(2,1)S(1)}, u32[]{:S(2)}, u32[]{:S(2)}) collective-permute-start(bf16[128,512]{1,0:T(8,128)(2,1)S(1)} %copy.21), channel_id=1, source_target_pairs={{0,1},{1,2},{2,3},{3,4},{4,5},{5,6},{6,7},{7,8},{8,9},{9,10},{10,1... | collective-permute-start | bytes 393224 | tf_op jit(solution)/shard_map/while/body/eval_jaxpr/ppermute | solution.py:14
  97.2 7.9 %collective-permute-start.1 = (f32[128,512]{1,0:T(8,128)}, f32[128,512]{1,0:T(8,128)S(1)}, u32[]{:S(2)}, u32[]{:S(2)}) collective-permute-start(f32[128,512]{1,0:T(8,128)} %fusion.42), channel_id=1, source_target_pairs={{0,1},{1,2},{2,3},{3,4},{4,5},{5,6},{6,7},{7,8},{8,9},{9,10},{10,1... | collective-permute-start | bytes 786440 | tf_op jit(solution)/shard_map/while/body/eval_jaxpr/ppermute | solution.py:14
  105.1 11.3 %collective-permute-start = (bf16[128,512]{1,0:T(8,128)(2,1)S(1)}, bf16[128,512]{1,0:T(8,128)(2,1)S(1)}, u32[]{:S(2)}, u32[]{:S(2)}) collective-permute-start(bf16[128,512]{1,0:T(8,128)(2,1)S(1)} %copy.21), channel_id=1, source_target_pairs={{0,1},{1,2},{2,3},{3,4},{4,5},{5,6},{6,7},{7,8},{8,9},{9,10},{10,1... | collective-permute-start | bytes 393224 | tf_op jit(solution)/shard_map/while/body/eval_jaxpr/ppermute | solution.py:14
  109.5 9.9 %collective-permute-start.1 = (f32[128,512]{1,0:T(8,128)}, f32[128,512]{1,0:T(8,128)S(1)}, u32[]{:S(2)}, u32[]{:S(2)}) collective-permute-start(f32[128,512]{1,0:T(8,128)} %fusion.42), channel_id=1, source_target_pairs={{0,1},{1,2},{2,3},{3,4},{4,5},{5,6},{6,7},{7,8},{8,9},{9,10},{10,1... | collective-permute-start | bytes 786440 | tf_op jit(solution)/shard_map/while/body/eval_jaxpr/ppermute | solution.py:14
  119.4 9.6 %collective-permute-start = (bf16[128,512]{1,0:T(8,128)(2,1)S(1)}, bf16[128,512]{1,0:T(8,128)(2,1)S(1)}, u32[]{:S(2)}, u32[]{:S(2)}) collective-permute-start(bf16[128,512]{1,0:T(8,128)(2,1)S(1)} %copy.21), channel_id=1, source_target_pairs={{0,1},{1,2},{2,3},{3,4},{4,5},{5,6},{6,7},{7,8},{8,9},{9,10},{10,1... | collective-permute-start | bytes 393224 | tf_op jit(solution)/shard_map/while/body/eval_jaxpr/ppermute | solution.py:14
  123.8 9.9 %collective-permute-start.1 = (f32[128,512]{1,0:T(8,128)}, f32[128,512]{1,0:T(8,128)S(1)}, u32[]{:S(2)}, u32[]{:S(2)}) collective-permute-start(f32[128,512]{1,0:T(8,128)} %fusion.42), channel_id=1, source_target_pairs={{0,1},{1,2},{2,3},{3,4},{4,5},{5,6},{6,7},{7,8},{8,9},{9,10},{10,1... | collective-permute-start | bytes 786440 | tf_op jit(solution)/shard_map/while/body/eval_jaxpr/ppermute | solution.py:14
  133.7 8.7 %collective-permute-start = (bf16[128,512]{1,0:T(8,128)(2,1)S(1)}, bf16[128,512]{1,0:T(8,128)(2,1)S(1)}, u32[]{:S(2)}, u32[]{:S(2)}) collective-permute-start(bf16[128,512]{1,0:T(8,128)(2,1)S(1)} %copy.21), channel_id=1, source_target_pairs={{0,1},{1,2},{2,3},{3,4},{4,5},{5,6},{6,7},{7,8},{8,9},{9,10},{10,1... | collective-permute-start | bytes 393224 | tf_op jit(solution)/shard_map/while/body/eval_jaxpr/ppermute | solution.py:14
  138.1 9.9 %collective-permute-start.1 = (f32[128,512]{1,0:T(8,128)}, f32[128,512]{1,0:T(8,128)S(1)}, u32[]{:S(2)}, u32[]{:S(2)}) collective-permute-start(f32[128,512]{1,0:T(8,128)} %fusion.42), channel_id=1, source_target_pairs={{0,1},{1,2},{2,3},{3,4},{4,5},{5,6},{6,7},{7,8},{8,9},{9,10},{10,1... | collective-permute-start | bytes 786440 | tf_op jit(solution)/shard_map/while/body/eval_jaxpr/ppermute | solution.py:14
  148.1 8.7 %collective-permute-start = (bf16[128,512]{1,0:T(8,128)(2,1)S(1)}, bf16[128,512]{1,0:T(8,128)(2,1)S(1)}, u32[]{:S(2)}, u32[]{:S(2)}) collective-permute-start(bf16[128,512]{1,0:T(8,128)(2,1)S(1)} %copy.21), channel_id=1, source_target_pairs={{0,1},{1,2},{2,3},{3,4},{4,5},{5,6},{6,7},{7,8},{8,9},{9,10},{10,1... | collective-permute-start | bytes 393224 | tf_op jit(solution)/shard_map/while/body/eval_jaxpr/ppermute | solution.py:14
  152.5 9.9 %collective-permute-start.1 = (f32[128,512]{1,0:T(8,128)}, f32[128,512]{1,0:T(8,128)S(1)}, u32[]{:S(2)}, u32[]{:S(2)}) collective-permute-start(f32[128,512]{1,0:T(8,128)} %fusion.42), channel_id=1, source_target_pairs={{0,1},{1,2},{2,3},{3,4},{4,5},{5,6},{6,7},{7,8},{8,9},{9,10},{10,1... | collective-permute-start | bytes 786440 | tf_op jit(solution)/shard_map/while/body/eval_jaxpr/ppermute | solution.py:14
  162.4 8.7 %collective-permute-start = (bf16[128,512]{1,0:T(8,128)(2,1)S(1)}, bf16[128,512]{1,0:T(8,128)(2,1)S(1)}, u32[]{:S(2)}, u32[]{:S(2)}) collective-permute-start(bf16[128,512]{1,0:T(8,128)(2,1)S(1)} %copy.21), channel_id=1, source_target_pairs={{0,1},{1,2},{2,3},{3,4},{4,5},{5,6},{6,7},{7,8},{8,9},{9,10},{10,1... | collective-permute-start | bytes 393224 | tf_op jit(solution)/shard_map/while/body/eval_jaxpr/ppermute | solution.py:14
  166.8 9.9 %collective-permute-start.1 = (f32[128,512]{1,0:T(8,128)}, f32[128,512]{1,0:T(8,128)S(1)}, u32[]{:S(2)}, u32[]{:S(2)}) collective-permute-start(f32[128,512]{1,0:T(8,128)} %fusion.42), channel_id=1, source_target_pairs={{0,1},{1,2},{2,3},{3,4},{4,5},{5,6},{6,7},{7,8},{8,9},{9,10},{10,1... | collective-permute-start | bytes 786440 | tf_op jit(solution)/shard_map/while/body/eval_jaxpr/ppermute | solution.py:14
  176.7 8.8 %collective-permute-start = (bf16[128,512]{1,0:T(8,128)(2,1)S(1)}, bf16[128,512]{1,0:T(8,128)(2,1)S(1)}, u32[]{:S(2)}, u32[]{:S(2)}) collective-permute-start(bf16[128,512]{1,0:T(8,128)(2,1)S(1)} %copy.21), channel_id=1, source_target_pairs={{0,1},{1,2},{2,3},{3,4},{4,5},{5,6},{6,7},{7,8},{8,9},{9,10},{10,1... | collective-permute-start | bytes 393224 | tf_op jit(solution)/shard_map/while/body/eval_jaxpr/ppermute | solution.py:14
  181.1 9.9 %collective-permute-start.1 = (f32[128,512]{1,0:T(8,128)}, f32[128,512]{1,0:T(8,128)S(1)}, u32[]{:S(2)}, u32[]{:S(2)}) collective-permute-start(f32[128,512]{1,0:T(8,128)} %fusion.42), channel_id=1, source_target_pairs={{0,1},{1,2},{2,3},{3,4},{4,5},{5,6},{6,7},{7,8},{8,9},{9,10},{10,1... | collective-permute-start | bytes 786440 | tf_op jit(solution)/shard_map/while/body/eval_jaxpr/ppermute | solution.py:14
  191.1 8.7 %collective-permute-start = (bf16[128,512]{1,0:T(8,128)(2,1)S(1)}, bf16[128,512]{1,0:T(8,128)(2,1)S(1)}, u32[]{:S(2)}, u32[]{:S(2)}) collective-permute-start(bf16[128,512]{1,0:T(8,128)(2,1)S(1)} %copy.21), channel_id=1, source_target_pairs={{0,1},{1,2},{2,3},{3,4},{4,5},{5,6},{6,7},{7,8},{8,9},{9,10},{10,1... | collective-permute-start | bytes 393224 | tf_op jit(solution)/shard_map/while/body/eval_jaxpr/ppermute | solution.py:14
  195.5 9.9 %collective-permute-start.1 = (f32[128,512]{1,0:T(8,128)}, f32[128,512]{1,0:T(8,128)S(1)}, u32[]{:S(2)}, u32[]{:S(2)}) collective-permute-start(f32[128,512]{1,0:T(8,128)} %fusion.42), channel_id=1, source_target_pairs={{0,1},{1,2},{2,3},{3,4},{4,5},{5,6},{6,7},{7,8},{8,9},{9,10},{10,1... | collective-permute-start | bytes 786440 | tf_op jit(solution)/shard_map/while/body/eval_jaxpr/ppermute | solution.py:14
  205.4 8.7 %collective-permute-start = (bf16[128,512]{1,0:T(8,128)(2,1)S(1)}, bf16[128,512]{1,0:T(8,128)(2,1)S(1)}, u32[]{:S(2)}, u32[]{:S(2)}) collective-permute-start(bf16[128,512]{1,0:T(8,128)(2,1)S(1)} %copy.21), channel_id=1, source_target_pairs={{0,1},{1,2},{2,3},{3,4},{4,5},{5,6},{6,7},{7,8},{8,9},{9,10},{10,1... | collective-permute-start | bytes 393224 | tf_op jit(solution)/shard_map/while/body/eval_jaxpr/ppermute | solution.py:14
  209.8 9.9 %collective-permute-start.1 = (f32[128,512]{1,0:T(8,128)}, f32[128,512]{1,0:T(8,128)S(1)}, u32[]{:S(2)}, u32[]{:S(2)}) collective-permute-start(f32[128,512]{1,0:T(8,128)} %fusion.42), channel_id=1, source_target_pairs={{0,1},{1,2},{2,3},{3,4},{4,5},{5,6},{6,7},{7,8},{8,9},{9,10},{10,1... | collective-permute-start | bytes 786440 | tf_op jit(solution)/shard_map/while/body/eval_jaxpr/ppermute | solution.py:14
  219.7 8.7 %collective-permute-start = (bf16[128,512]{1,0:T(8,128)(2,1)S(1)}, bf16[128,512]{1,0:T(8,128)(2,1)S(1)}, u32[]{:S(2)}, u32[]{:S(2)}) collective-permute-start(bf16[128,512]{1,0:T(8,128)(2,1)S(1)} %copy.21), channel_id=1, source_target_pairs={{0,1},{1,2},{2,3},{3,4},{4,5},{5,6},{6,7},{7,8},{8,9},{9,10},{10,1... | collective-permute-start | bytes 393224 | tf_op jit(solution)/shard_map/while/body/eval_jaxpr/ppermute | solution.py:14
  224.1 9.9 %collective-permute-start.1 = (f32[128,512]{1,0:T(8,128)}, f32[128,512]{1,0:T(8,128)S(1)}, u32[]{:S(2)}, u32[]{:S(2)}) collective-permute-start(f32[128,512]{1,0:T(8,128)} %fusion.42), channel_id=1, source_target_pairs={{0,1},{1,2},{2,3},{3,4},{4,5},{5,6},{6,7},{7,8},{8,9},{9,10},{10,1... | collective-permute-start | bytes 786440 | tf_op jit(solution)/shard_map/while/body/eval_jaxpr/ppermute | solution.py:14
  234.1 8.7 %collective-permute-start = (bf16[128,512]{1,0:T(8,128)(2,1)S(1)}, bf16[128,512]{1,0:T(8,128)(2,1)S(1)}, u32[]{:S(2)}, u32[]{:S(2)}) collective-permute-start(bf16[128,512]{1,0:T(8,128)(2,1)S(1)} %copy.21), channel_id=1, source_target_pairs={{0,1},{1,2},{2,3},{3,4},{4,5},{5,6},{6,7},{7,8},{8,9},{9,10},{10,1... | collective-permute-start | bytes 393224 | tf_op jit(solution)/shard_map/while/body/eval_jaxpr/ppermute | solution.py:14
  238.5 9.9 %collective-permute-start.1 = (f32[128,512]{1,0:T(8,128)}, f32[128,512]{1,0:T(8,128)S(1)}, u32[]{:S(2)}, u32[]{:S(2)}) collective-permute-start(f32[128,512]{1,0:T(8,128)} %fusion.42), channel_id=1, source_target_pairs={{0,1},{1,2},{2,3},{3,4},{4,5},{5,6},{6,7},{7,8},{8,9},{9,10},{10,1... | collective-permute-start | bytes 786440 | tf_op jit(solution)/shard_map/while/body/eval_jaxpr/ppermute | solution.py:14
  248.4 8.7 %collective-permute-start = (bf16[128,512]{1,0:T(8,128)(2,1)S(1)}, bf16[128,512]{1,0:T(8,128)(2,1)S(1)}, u32[]{:S(2)}, u32[]{:S(2)}) collective-permute-start(bf16[128,512]{1,0:T(8,128)(2,1)S(1)} %copy.21), channel_id=1, source_target_pairs={{0,1},{1,2},{2,3},{3,4},{4,5},{5,6},{6,7},{7,8},{8,9},{9,10},{10,1... | collective-permute-start | bytes 393224 | tf_op jit(solution)/shard_map/while/body/eval_jaxpr/ppermute | solution.py:14
  252.8 9.9 %collective-permute-start.1 = (f32[128,512]{1,0:T(8,128)}, f32[128,512]{1,0:T(8,128)S(1)}, u32[]{:S(2)}, u32[]{:S(2)}) collective-permute-start(f32[128,512]{1,0:T(8,128)} %fusion.42), channel_id=1, source_target_pairs={{0,1},{1,2},{2,3},{3,4},{4,5},{5,6},{6,7},{7,8},{8,9},{9,10},{10,1... | collective-permute-start | bytes 786440 | tf_op jit(solution)/shard_map/while/body/eval_jaxpr/ppermute | solution.py:14
  262.7 8.7 %collective-permute-start = (bf16[128,512]{1,0:T(8,128)(2,1)S(1)}, bf16[128,512]{1,0:T(8,128)(2,1)S(1)}, u32[]{:S(2)}, u32[]{:S(2)}) collective-permute-start(bf16[128,512]{1,0:T(8,128)(2,1)S(1)} %copy.21), channel_id=1, source_target_pairs={{0,1},{1,2},{2,3},{3,4},{4,5},{5,6},{6,7},{7,8},{8,9},{9,10},{10,1... | collective-permute-start | bytes 393224 | tf_op jit(solution)/shard_map/while/body/eval_jaxpr/ppermute | solution.py:14
  267.1 9.9 %collective-permute-start.1 = (f32[128,512]{1,0:T(8,128)}, f32[128,512]{1,0:T(8,128)S(1)}, u32[]{:S(2)}, u32[]{:S(2)}) collective-permute-start(f32[128,512]{1,0:T(8,128)} %fusion.42), channel_id=1, source_target_pairs={{0,1},{1,2},{2,3},{3,4},{4,5},{5,6},{6,7},{7,8},{8,9},{9,10},{10,1... | collective-permute-start | bytes 786440 | tf_op jit(solution)/shard_map/while/body/eval_jaxpr/ppermute | solution.py:14
  277.1 8.7 %collective-permute-start = (bf16[128,512]{1,0:T(8,128)(2,1)S(1)}, bf16[128,512]{1,0:T(8,128)(2,1)S(1)}, u32[]{:S(2)}, u32[]{:S(2)}) collective-permute-start(bf16[128,512]{1,0:T(8,128)(2,1)S(1)} %copy.21), channel_id=1, source_target_pairs={{0,1},{1,2},{2,3},{3,4},{4,5},{5,6},{6,7},{7,8},{8,9},{9,10},{10,1... | collective-permute-start | bytes 393224 | tf_op jit(solution)/shard_map/while/body/eval_jaxpr/ppermute | solution.py:14
  281.5 9.9 %collective-permute-start.1 = (f32[128,512]{1,0:T(8,128)}, f32[128,512]{1,0:T(8,128)S(1)}, u32[]{:S(2)}, u32[]{:S(2)}) collective-permute-start(f32[128,512]{1,0:T(8,128)} %fusion.42), channel_id=1, source_target_pairs={{0,1},{1,2},{2,3},{3,4},{4,5},{5,6},{6,7},{7,8},{8,9},{9,10},{10,1... | collective-permute-start | bytes 786440 | tf_op jit(solution)/shard_map/while/body/eval_jaxpr/ppermute | solution.py:14
  291.4 8.7 %collective-permute-start = (bf16[128,512]{1,0:T(8,128)(2,1)S(1)}, bf16[128,512]{1,0:T(8,128)(2,1)S(1)}, u32[]{:S(2)}, u32[]{:S(2)}) collective-permute-start(bf16[128,512]{1,0:T(8,128)(2,1)S(1)} %copy.21), channel_id=1, source_target_pairs={{0,1},{1,2},{2,3},{3,4},{4,5},{5,6},{6,7},{7,8},{8,9},{9,10},{10,1... | collective-permute-start | bytes 393224 | tf_op jit(solution)/shard_map/while/body/eval_jaxpr/ppermute | solution.py:14
  295.8 9.9 %collective-permute-start.1 = (f32[128,512]{1,0:T(8,128)}, f32[128,512]{1,0:T(8,128)S(1)}, u32[]{:S(2)}, u32[]{:S(2)}) collective-permute-start(f32[128,512]{1,0:T(8,128)} %fusion.42), channel_id=1, source_target_pairs={{0,1},{1,2},{2,3},{3,4},{4,5},{5,6},{6,7},{7,8},{8,9},{9,10},{10,1... | collective-permute-start | bytes 786440 | tf_op jit(solution)/shard_map/while/body/eval_jaxpr/ppermute | solution.py:14
  305.7 8.7 %collective-permute-start = (bf16[128,512]{1,0:T(8,128)(2,1)S(1)}, bf16[128,512]{1,0:T(8,128)(2,1)S(1)}, u32[]{:S(2)}, u32[]{:S(2)}) collective-permute-start(bf16[128,512]{1,0:T(8,128)(2,1)S(1)} %copy.21), channel_id=1, source_target_pairs={{0,1},{1,2},{2,3},{3,4},{4,5},{5,6},{6,7},{7,8},{8,9},{9,10},{10,1... | collective-permute-start | bytes 393224 | tf_op jit(solution)/shard_map/while/body/eval_jaxpr/ppermute | solution.py:14
  310.1 9.9 %collective-permute-start.1 = (f32[128,512]{1,0:T(8,128)}, f32[128,512]{1,0:T(8,128)S(1)}, u32[]{:S(2)}, u32[]{:S(2)}) collective-permute-start(f32[128,512]{1,0:T(8,128)} %fusion.42), channel_id=1, source_target_pairs={{0,1},{1,2},{2,3},{3,4},{4,5},{5,6},{6,7},{7,8},{8,9},{9,10},{10,1... | collective-permute-start | bytes 786440 | tf_op jit(solution)/shard_map/while/body/eval_jaxpr/ppermute | solution.py:14
  320.1 8.7 %collective-permute-start = (bf16[128,512]{1,0:T(8,128)(2,1)S(1)}, bf16[128,512]{1,0:T(8,128)(2,1)S(1)}, u32[]{:S(2)}, u32[]{:S(2)}) collective-permute-start(bf16[128,512]{1,0:T(8,128)(2,1)S(1)} %copy.21), channel_id=1, source_target_pairs={{0,1},{1,2},{2,3},{3,4},{4,5},{5,6},{6,7},{7,8},{8,9},{9,10},{10,1... | collective-permute-start | bytes 393224 | tf_op jit(solution)/shard_map/while/body/eval_jaxpr/ppermute | solution.py:14
  324.5 9.9 %collective-permute-start.1 = (f32[128,512]{1,0:T(8,128)}, f32[128,512]{1,0:T(8,128)S(1)}, u32[]{:S(2)}, u32[]{:S(2)}) collective-permute-start(f32[128,512]{1,0:T(8,128)} %fusion.42), channel_id=1, source_target_pairs={{0,1},{1,2},{2,3},{3,4},{4,5},{5,6},{6,7},{7,8},{8,9},{9,10},{10,1... | collective-permute-start | bytes 786440 | tf_op jit(solution)/shard_map/while/body/eval_jaxpr/ppermute | solution.py:14
  334.4 8.7 %collective-permute-start = (bf16[128,512]{1,0:T(8,128)(2,1)S(1)}, bf16[128,512]{1,0:T(8,128)(2,1)S(1)}, u32[]{:S(2)}, u32[]{:S(2)}) collective-permute-start(bf16[128,512]{1,0:T(8,128)(2,1)S(1)} %copy.21), channel_id=1, source_target_pairs={{0,1},{1,2},{2,3},{3,4},{4,5},{5,6},{6,7},{7,8},{8,9},{9,10},{10,1... | collective-permute-start | bytes 393224 | tf_op jit(solution)/shard_map/while/body/eval_jaxpr/ppermute | solution.py:14
  338.8 9.9 %collective-permute-start.1 = (f32[128,512]{1,0:T(8,128)}, f32[128,512]{1,0:T(8,128)S(1)}, u32[]{:S(2)}, u32[]{:S(2)}) collective-permute-start(f32[128,512]{1,0:T(8,128)} %fusion.42), channel_id=1, source_target_pairs={{0,1},{1,2},{2,3},{3,4},{4,5},{5,6},{6,7},{7,8},{8,9},{9,10},{10,1... | collective-permute-start | bytes 786440 | tf_op jit(solution)/shard_map/while/body/eval_jaxpr/ppermute | solution.py:14
  348.7 8.7 %collective-permute-start = (bf16[128,512]{1,0:T(8,128)(2,1)S(1)}, bf16[128,512]{1,0:T(8,128)(2,1)S(1)}, u32[]{:S(2)}, u32[]{:S(2)}) collective-permute-start(bf16[128,512]{1,0:T(8,128)(2,1)S(1)} %copy.21), channel_id=1, source_target_pairs={{0,1},{1,2},{2,3},{3,4},{4,5},{5,6},{6,7},{7,8},{8,9},{9,10},{10,1... | collective-permute-start | bytes 393224 | tf_op jit(solution)/shard_map/while/body/eval_jaxpr/ppermute | solution.py:14
  353.1 9.9 %collective-permute-start.1 = (f32[128,512]{1,0:T(8,128)}, f32[128,512]{1,0:T(8,128)S(1)}, u32[]{:S(2)}, u32[]{:S(2)}) collective-permute-start(f32[128,512]{1,0:T(8,128)} %fusion.42), channel_id=1, source_target_pairs={{0,1},{1,2},{2,3},{3,4},{4,5},{5,6},{6,7},{7,8},{8,9},{9,10},{10,1... | collective-permute-start | bytes 786440 | tf_op jit(solution)/shard_map/while/body/eval_jaxpr/ppermute | solution.py:14
  363.1 8.7 %collective-permute-start = (bf16[128,512]{1,0:T(8,128)(2,1)S(1)}, bf16[128,512]{1,0:T(8,128)(2,1)S(1)}, u32[]{:S(2)}, u32[]{:S(2)}) collective-permute-start(bf16[128,512]{1,0:T(8,128)(2,1)S(1)} %copy.21), channel_id=1, source_target_pairs={{0,1},{1,2},{2,3},{3,4},{4,5},{5,6},{6,7},{7,8},{8,9},{9,10},{10,1... | collective-permute-start | bytes 393224 | tf_op jit(solution)/shard_map/while/body/eval_jaxpr/ppermute | solution.py:14
  367.5 9.9 %collective-permute-start.1 = (f32[128,512]{1,0:T(8,128)}, f32[128,512]{1,0:T(8,128)S(1)}, u32[]{:S(2)}, u32[]{:S(2)}) collective-permute-start(f32[128,512]{1,0:T(8,128)} %fusion.42), channel_id=1, source_target_pairs={{0,1},{1,2},{2,3},{3,4},{4,5},{5,6},{6,7},{7,8},{8,9},{9,10},{10,1... | collective-permute-start | bytes 786440 | tf_op jit(solution)/shard_map/while/body/eval_jaxpr/ppermute | solution.py:14
  377.4 8.7 %collective-permute-start = (bf16[128,512]{1,0:T(8,128)(2,1)S(1)}, bf16[128,512]{1,0:T(8,128)(2,1)S(1)}, u32[]{:S(2)}, u32[]{:S(2)}) collective-permute-start(bf16[128,512]{1,0:T(8,128)(2,1)S(1)} %copy.21), channel_id=1, source_target_pairs={{0,1},{1,2},{2,3},{3,4},{4,5},{5,6},{6,7},{7,8},{8,9},{9,10},{10,1... | collective-permute-start | bytes 393224 | tf_op jit(solution)/shard_map/while/body/eval_jaxpr/ppermute | solution.py:14
  381.8 9.9 %collective-permute-start.1 = (f32[128,512]{1,0:T(8,128)}, f32[128,512]{1,0:T(8,128)S(1)}, u32[]{:S(2)}, u32[]{:S(2)}) collective-permute-start(f32[128,512]{1,0:T(8,128)} %fusion.42), channel_id=1, source_target_pairs={{0,1},{1,2},{2,3},{3,4},{4,5},{5,6},{6,7},{7,8},{8,9},{9,10},{10,1... | collective-permute-start | bytes 786440 | tf_op jit(solution)/shard_map/while/body/eval_jaxpr/ppermute | solution.py:14
  391.7 8.7 %collective-permute-start = (bf16[128,512]{1,0:T(8,128)(2,1)S(1)}, bf16[128,512]{1,0:T(8,128)(2,1)S(1)}, u32[]{:S(2)}, u32[]{:S(2)}) collective-permute-start(bf16[128,512]{1,0:T(8,128)(2,1)S(1)} %copy.21), channel_id=1, source_target_pairs={{0,1},{1,2},{2,3},{3,4},{4,5},{5,6},{6,7},{7,8},{8,9},{9,10},{10,1... | collective-permute-start | bytes 393224 | tf_op jit(solution)/shard_map/while/body/eval_jaxpr/ppermute | solution.py:14
  396.1 9.9 %collective-permute-start.1 = (f32[128,512]{1,0:T(8,128)}, f32[128,512]{1,0:T(8,128)S(1)}, u32[]{:S(2)}, u32[]{:S(2)}) collective-permute-start(f32[128,512]{1,0:T(8,128)} %fusion.42), channel_id=1, source_target_pairs={{0,1},{1,2},{2,3},{3,4},{4,5},{5,6},{6,7},{7,8},{8,9},{9,10},{10,1... | collective-permute-start | bytes 786440 | tf_op jit(solution)/shard_map/while/body/eval_jaxpr/ppermute | solution.py:14
  406.1 8.7 %collective-permute-start = (bf16[128,512]{1,0:T(8,128)(2,1)S(1)}, bf16[128,512]{1,0:T(8,128)(2,1)S(1)}, u32[]{:S(2)}, u32[]{:S(2)}) collective-permute-start(bf16[128,512]{1,0:T(8,128)(2,1)S(1)} %copy.21), channel_id=1, source_target_pairs={{0,1},{1,2},{2,3},{3,4},{4,5},{5,6},{6,7},{7,8},{8,9},{9,10},{10,1... | collective-permute-start | bytes 393224 | tf_op jit(solution)/shard_map/while/body/eval_jaxpr/ppermute | solution.py:14
  410.5 9.9 %collective-permute-start.1 = (f32[128,512]{1,0:T(8,128)}, f32[128,512]{1,0:T(8,128)S(1)}, u32[]{:S(2)}, u32[]{:S(2)}) collective-permute-start(f32[128,512]{1,0:T(8,128)} %fusion.42), channel_id=1, source_target_pairs={{0,1},{1,2},{2,3},{3,4},{4,5},{5,6},{6,7},{7,8},{8,9},{9,10},{10,1... | collective-permute-start | bytes 786440 | tf_op jit(solution)/shard_map/while/body/eval_jaxpr/ppermute | solution.py:14
  420.4 8.7 %collective-permute-start = (bf16[128,512]{1,0:T(8,128)(2,1)S(1)}, bf16[128,512]{1,0:T(8,128)(2,1)S(1)}, u32[]{:S(2)}, u32[]{:S(2)}) collective-permute-start(bf16[128,512]{1,0:T(8,128)(2,1)S(1)} %copy.21), channel_id=1, source_target_pairs={{0,1},{1,2},{2,3},{3,4},{4,5},{5,6},{6,7},{7,8},{8,9},{9,10},{10,1... | collective-permute-start | bytes 393224 | tf_op jit(solution)/shard_map/while/body/eval_jaxpr/ppermute | solution.py:14
  424.8 9.9 %collective-permute-start.1 = (f32[128,512]{1,0:T(8,128)}, f32[128,512]{1,0:T(8,128)S(1)}, u32[]{:S(2)}, u32[]{:S(2)}) collective-permute-start(f32[128,512]{1,0:T(8,128)} %fusion.42), channel_id=1, source_target_pairs={{0,1},{1,2},{2,3},{3,4},{4,5},{5,6},{6,7},{7,8},{8,9},{9,10},{10,1... | collective-permute-start | bytes 786440 | tf_op jit(solution)/shard_map/while/body/eval_jaxpr/ppermute | solution.py:14
  434.7 8.7 %collective-permute-start = (bf16[128,512]{1,0:T(8,128)(2,1)S(1)}, bf16[128,512]{1,0:T(8,128)(2,1)S(1)}, u32[]{:S(2)}, u32[]{:S(2)}) collective-permute-start(bf16[128,512]{1,0:T(8,128)(2,1)S(1)} %copy.21), channel_id=1, source_target_pairs={{0,1},{1,2},{2,3},{3,4},{4,5},{5,6},{6,7},{7,8},{8,9},{9,10},{10,1... | collective-permute-start | bytes 393224 | tf_op jit(solution)/shard_map/while/body/eval_jaxpr/ppermute | solution.py:14
  439.1 9.9 %collective-permute-start.1 = (f32[128,512]{1,0:T(8,128)}, f32[128,512]{1,0:T(8,128)S(1)}, u32[]{:S(2)}, u32[]{:S(2)}) collective-permute-start(f32[128,512]{1,0:T(8,128)} %fusion.42), channel_id=1, source_target_pairs={{0,1},{1,2},{2,3},{3,4},{4,5},{5,6},{6,7},{7,8},{8,9},{9,10},{10,1... | collective-permute-start | bytes 786440 | tf_op jit(solution)/shard_map/while/body/eval_jaxpr/ppermute | solution.py:14
  449.1 8.7 %collective-permute-start = (bf16[128,512]{1,0:T(8,128)(2,1)S(1)}, bf16[128,512]{1,0:T(8,128)(2,1)S(1)}, u32[]{:S(2)}, u32[]{:S(2)}) collective-permute-start(bf16[128,512]{1,0:T(8,128)(2,1)S(1)} %copy.21), channel_id=1, source_target_pairs={{0,1},{1,2},{2,3},{3,4},{4,5},{5,6},{6,7},{7,8},{8,9},{9,10},{10,1... | collective-permute-start | bytes 393224 | tf_op jit(solution)/shard_map/while/body/eval_jaxpr/ppermute | solution.py:14
  453.5 9.9 %collective-permute-start.1 = (f32[128,512]{1,0:T(8,128)}, f32[128,512]{1,0:T(8,128)S(1)}, u32[]{:S(2)}, u32[]{:S(2)}) collective-permute-start(f32[128,512]{1,0:T(8,128)} %fusion.42), channel_id=1, source_target_pairs={{0,1},{1,2},{2,3},{3,4},{4,5},{5,6},{6,7},{7,8},{8,9},{9,10},{10,1... | collective-permute-start | bytes 786440 | tf_op jit(solution)/shard_map/while/body/eval_jaxpr/ppermute | solution.py:14
  463.4 8.7 %collective-permute-start = (bf16[128,512]{1,0:T(8,128)(2,1)S(1)}, bf16[128,512]{1,0:T(8,128)(2,1)S(1)}, u32[]{:S(2)}, u32[]{:S(2)}) collective-permute-start(bf16[128,512]{1,0:T(8,128)(2,1)S(1)} %copy.21), channel_id=1, source_target_pairs={{0,1},{1,2},{2,3},{3,4},{4,5},{5,6},{6,7},{7,8},{8,9},{9,10},{10,1... | collective-permute-start | bytes 393224 | tf_op jit(solution)/shard_map/while/body/eval_jaxpr/ppermute | solution.py:14
  467.8 9.9 %collective-permute-start.1 = (f32[128,512]{1,0:T(8,128)}, f32[128,512]{1,0:T(8,128)S(1)}, u32[]{:S(2)}, u32[]{:S(2)}) collective-permute-start(f32[128,512]{1,0:T(8,128)} %fusion.42), channel_id=1, source_target_pairs={{0,1},{1,2},{2,3},{3,4},{4,5},{5,6},{6,7},{7,8},{8,9},{9,10},{10,1... | collective-permute-start | bytes 786440 | tf_op jit(solution)/shard_map/while/body/eval_jaxpr/ppermute | solution.py:14
  477.7 8.7 %collective-permute-start = (bf16[128,512]{1,0:T(8,128)(2,1)S(1)}, bf16[128,512]{1,0:T(8,128)(2,1)S(1)}, u32[]{:S(2)}, u32[]{:S(2)}) collective-permute-start(bf16[128,512]{1,0:T(8,128)(2,1)S(1)} %copy.21), channel_id=1, source_target_pairs={{0,1},{1,2},{2,3},{3,4},{4,5},{5,6},{6,7},{7,8},{8,9},{9,10},{10,1... | collective-permute-start | bytes 393224 | tf_op jit(solution)/shard_map/while/body/eval_jaxpr/ppermute | solution.py:14
  482.1 9.9 %collective-permute-start.1 = (f32[128,512]{1,0:T(8,128)}, f32[128,512]{1,0:T(8,128)S(1)}, u32[]{:S(2)}, u32[]{:S(2)}) collective-permute-start(f32[128,512]{1,0:T(8,128)} %fusion.42), channel_id=1, source_target_pairs={{0,1},{1,2},{2,3},{3,4},{4,5},{5,6},{6,7},{7,8},{8,9},{9,10},{10,1... | collective-permute-start | bytes 786440 | tf_op jit(solution)/shard_map/while/body/eval_jaxpr/ppermute | solution.py:14
  494.1 9.8 %collective-permute-start.2 = (f32[128,512]{1,0:T(8,128)S(1)}, f32[128,512]{1,0:T(8,128)S(1)}, u32[]{:S(2)}, u32[]{:S(2)}) collective-permute-start(f32[128,512]{1,0:T(8,128)S(1)} %fusion.15), channel_id=1, source_target_pairs={{0,1},{1,2},{2,3},{3,4},{4,5},{5,6},{6,7},{7,8},{8,9},{9,10},{10,1... | collective-permute-start | bytes 786440 | tf_op jit(solution)/shard_map/ppermute | solution.py:14
  (6 other events, 213.5 us)
Sparse Core Ops, SparseCore 0:
  504.7 94.2 reduce-scatter.1
where the time goes:
time: 610 us; the launch traced here: 607 us
  waiting for transfers between devices  248 us (41%)
  other arithmetic  149 us (24%)
  matrix products  87.9 us (14%)
  blocking collectives  46.2 us (8%)
  local copies, waits for them, and re-layouts  45.8 us (8%)
  between operations  14.2 us (2%)
  starting transfers between devices  13.6 us (2%)
    ppermute x63, waiting for transfers between devices, passed_along(): return lax.ppermute(value, axis, pairs)  159 us
    scatter-add x32, other arithmetic, padded_work(): region_totals = region_totals.at[rows_now].add(update)  124 us
    reduce_scatter x1, waiting for transfers between devices, on_device(): lax.psum_scatter(grad_home, 'row', scatter_dimension=0, tiled=True)  89.8 us
    all_gather x1, blocking collectives, on_device(): panel_start = lax.all_gather(item_factors, 'row', axis=1, tiled=True)[0]  46.2 us
    dot_general x32, matrix products, padded_work(): jnp.einsum('sik,jk->sij', chosen, panel_now, preferred_element_type=jnp.f...  43.1 us
    dot_general x32, matrix products, padded_work(): jnp.einsum('sij,sik->jk', residual, chosen, preferred_element_type=jnp.fl...  32.8 us
    gather x32, local copies, waits for them, and re-layouts, padded_work(): chosen = jnp.take(region_blocks, rows_now, axis=0)  21.3 us
    dynamic_slice x32, local copies, waits for them, and re-layouts, padded_work(): count_now = lax.dynamic_index_in_dim(live_counts, column, 0, keepdims=False)  20.1 us
  transfers between devices with their start and end apart: 64, of which 33 were waited for; matrix products, arithmetic and copies ran while one was open for 44% of the time, Pallas kernels for 0%

commit v1 on v0

--- a/solution.py
+++ b/solution.py
@@ -6,6 +6,11 @@
 region_rate = 0.05
 item_rate = 0.01
 decay_rate = 0.1
+
+
+def swapped_in(x, mesh_axis, dim):
+    sent = jnp.stack([x] * lax.axis_size(mesh_axis))
+    return jnp.concatenate(lax.all_to_all(sent, mesh_axis, 0, 0), axis=dim)
 
 
 def passed_along(value, axis, steps):
@@ -30,7 +35,7 @@
     row_lists = block_rows[0]
     live_counts = counts[0]
     slot_ids = jnp.arange(slot_total, dtype=jnp.int32)
-    panel_start = lax.all_gather(item_factors, "row", axis=1, tiled=True)[0]
+    panel_start = swapped_in(item_factors, "row", 1)[0]
     region_zero = jnp.zeros((row_blocks, block_size, factor_width), jnp.float32)
     item_zero = jnp.zeros((block_size, factor_width), jnp.float32)
 

time: 610 us -> 580 us (0.951)
  blocking collectives: 46.2 us -> 0 us
  starting transfers between devices: 13.6 us -> 25.2 us
    all_gather x1 -> x0, blocking collectives: 46.2 us -> none  [on_device(): panel_start = lax.all_gather(item_factors, 'row', axis=1, tiled=True)[0]]
    all_to_all x0 -> x1, starting transfers between devices: none -> 11.1 us  [swapped_in(): return jnp.concatenate(lax.all_to_all(sent, mesh_axis, 0, 0), axis=dim)]
  transfers between devices with their start and end apart: 64 -> 65, of which waited for: 33 -> 34; matrix products, arithmetic and copies ran while one was open for 44% -> 48% of each run, Pallas kernels for 0% -> 0%
where the time goes in v1:
time: 580 us; the launch traced here: 577 us
  waiting for transfers between devices  248 us (43%)
  other arithmetic  150 us (26%)
  matrix products  88.9 us (15%)
  local copies, waits for them, and re-layouts  48.7 us (8%)
  starting transfers between devices  25.2 us (4%)
  between operations  14.1 us (2%)
    ppermute x63, waiting for transfers between devices, passed_along(): return lax.ppermute(value, axis, pairs)  159 us
    scatter-add x32, other arithmetic, padded_work(): region_totals = region_totals.at[rows_now].add(update)  124 us
    reduce_scatter x1, waiting for transfers between devices, on_device(): lax.psum_scatter(grad_home, 'row', scatter_dimension=0, tiled=True)  84.7 us
    dot_general x32, matrix products, padded_work(): jnp.einsum('sik,jk->sij', chosen, panel_now, preferred_element_type=jnp.f...  43.1 us
    dot_general x32, matrix products, padded_work(): jnp.einsum('sij,sik->jk', residual, chosen, preferred_element_type=jnp.fl...  32.9 us
    dynamic_slice x32, local copies, waits for them, and re-layouts, padded_work(): count_now = lax.dynamic_index_in_dim(live_counts, column, 0, keepdims=False)  21.5 us
    gather x32, local copies, waits for them, and re-layouts, padded_work(): chosen = jnp.take(region_blocks, rows_now, axis=0)  21.3 us
    lt x31, other arithmetic, padded_work(): present = slot_ids < count_now  20.9 us
  transfers between devices with their start and end apart: 65, of which 34 were waited for; matrix products, arithmetic and copies ran while one was open for 48% of the time, Pallas kernels for 0%

profile of v1, /device:TPU:8, one launch (start us, length us, event | category | flops | bytes accessed | tf_op | source)
XLA Modules:
  0.0 577.4 jit_solution(1041018516621986855)
XLA Ops:
  8.6 11.1 %all-to-all-start = ((bf16[8,1,16,512]{3,2,1,0:T(8,128)(2,1)}), bf16[8,1,16,512]{3,2,1,0:T(8,128)(2,1)S(1)}, u32[]{:S(2)}, u32[]{:S(2)}) async-start(bf16[8,1,16,512]{3,2,1,0:T(8,128)(2,1)} %stack.2), calls=%async_computation | async-start | bytes 262144 | tf_op jit(solution)/shard_map/all_to_all | solution.py:13
  26.1 4.0 all-to-all-done
  31.7 433.0 %while.20 = (s32[]{:T(128)}, bf16[128,512]{1,0:T(8,128)(2,1)S(1)}, f32[128,512]{1,0:T(8,128)S(1)}, f32[8,128,512]{2,1,0:T(8,128)}, s32[]{:T(128)}, /*index=5*/s3...) while((s32[]{:T(128)}, bf16[128,512]{1,0:T(8,128)(2,1)S(1)}, ...), condition=%wide.region_2.4_spmd.clone, body=%wide.region_0.3_spmd.clone.sunk | while | flops 303629376 | bytes 12849738 | solution.py:70
  38.2 3.9 scatter_fusion
  48.7 3.9 scatter_fusion
  59.2 3.9 scatter_fusion
  70.7 3.9 scatter_fusion
  80.1 2.9 collective-permute-start.1
  83.3 3.9 scatter_fusion
  95.9 3.9 scatter_fusion
  99.8 4.6 collective-permute-done.1
  109.3 3.9 scatter_fusion
  113.2 5.7 collective-permute-done.1
  123.7 3.9 scatter_fusion
  127.6 5.6 collective-permute-done.1
  138.1 3.9 scatter_fusion
  142.0 5.7 collective-permute-done.1
  152.5 3.9 scatter_fusion
  156.5 5.6 collective-permute-done.1
  166.9 3.9 scatter_fusion
  170.8 5.7 collective-permute-done.1
  181.4 3.9 scatter_fusion
  185.3 5.6 collective-permute-done.1
  195.8 3.9 scatter_fusion
  199.7 5.7 collective-permute-done.1
  210.2 3.9 scatter_fusion
  214.1 5.6 collective-permute-done.1
  224.6 3.9 scatter_fusion
  228.5 5.7 collective-permute-done.1
  239.0 3.9 scatter_fusion
  242.9 5.6 collective-permute-done.1
  253.4 3.9 scatter_fusion
  257.3 5.7 collective-permute-done.1
  267.8 4.0 scatter_fusion
  271.8 5.6 collective-permute-done.1
  282.2 3.9 scatter_fusion
  286.1 5.7 collective-permute-done.1
  296.7 3.9 scatter_fusion
  300.6 5.6 collective-permute-done.1
  311.1 3.9 scatter_fusion
  315.0 5.7 collective-permute-done.1
  325.5 3.9 scatter_fusion
  329.4 5.6 collective-permute-done.1
  339.9 3.9 scatter_fusion
  343.8 5.7 collective-permute-done.1
  354.3 3.9 scatter_fusion
  358.2 5.6 collective-permute-done.1
  368.7 3.9 scatter_fusion
  372.6 5.7 collective-permute-done.1
  383.1 3.9 scatter_fusion
  387.0 5.6 collective-permute-done.1
  397.5 3.9 scatter_fusion
  401.4 5.7 collective-permute-done.1
  412.0 3.9 scatter_fusion
  415.9 5.6 collective-permute-done.1
  426.4 3.9 scatter_fusion
  430.3 5.7 collective-permute-done.1
  440.8 3.9 scatter_fusion
  444.7 5.6 collective-permute-done.1
  455.2 3.9 scatter_fusion
  459.1 5.7 collective-permute-done.1
  467.1 9.7 %collective-permute-done.2 = f32[128,512]{1,0:T(8,128)S(1)} collective-permute-done((f32[128,512]{1,0:T(8,128)S(1)}, f32[128,512]{1,0:T(8,128)S(1)}, u32[]{:S(2)}, u32[]{:S(2)}) %collective-permute-start.2) | collective-permute-done | bytes 262176 | tf_op jit(solution)/shard_map/ppermute | solution.py:19
  479.9 2.9 scatter_fusion.1
  484.5 84.7 %reduce-scatter.2.cloned.1.call-done = f32[16,512]{1,0:T(8,128)} async-done(((f32[128,512]{1,0:T(8,128)}), f32[16,512]{1,0:T(8,128)}) %reduce-scatter.2.cloned.1.call-update) | async-done | bytes 32784 | tf_op jit(solution)/shard_map/reduce_scatter | solution.py:75
  (440 shorter events, 178.9 us)
Async XLA Ops:
  8.6 21.5 %all-to-all-start = ((bf16[8,1,16,512]{3,2,1,0:T(8,128)(2,1)}), bf16[8,1,16,512]{3,2,1,0:T(8,128)(2,1)S(1)}, u32[]{:S(2)}, u32[]{:S(2)}) async-start(bf16[8,1,16,512]{3,2,1,0:T(8,128)(2,1)} %stack.2), calls=%async_computation | async-start | bytes 262144 | tf_op jit(solution)/shard_map/all_to_all | solution.py:13
  19.6 549.6 %reduce-scatter.2.cloned.1.call-start = ((), (), s32[]{:S(2)}) async-start(), calls=%async_computation.2 | async-start | bytes 294912 | tf_op jit(solution)/shard_map/reduce_scatter | solution.py:75
  31.7 10.4 %collective-permute-start = (bf16[128,512]{1,0:T(8,128)(2,1)S(1)}, bf16[128,512]{1,0:T(8,128)(2,1)S(1)}, u32[]{:S(2)}, u32[]{:S(2)}) collective-permute-start(bf16[128,512]{1,0:T(8,128)(2,1)S(1)} %copy.24), channel_id=1, source_target_pairs={{0,1},{1,2},{2,3},{3,4},{4,5},{5,6},{6,7},{7,8},{8,9},{9,10},{10,1... | collective-permute-start | bytes 393224 | tf_op jit(solution)/shard_map/while/body/eval_jaxpr/ppermute | solution.py:19
  36.2 6.0 %collective-permute-start.1 = (f32[128,512]{1,0:T(8,128)}, f32[128,512]{1,0:T(8,128)S(1)}, u32[]{:S(2)}, u32[]{:S(2)}) collective-permute-start(f32[128,512]{1,0:T(8,128)} %fusion.42), channel_id=1, source_target_pairs={{0,1},{1,2},{2,3},{3,4},{4,5},{5,6},{6,7},{7,8},{8,9},{9,10},{10,1... | collective-permute-start | bytes 786440 | tf_op jit(solution)/shard_map/while/body/eval_jaxpr/ppermute | solution.py:19
  42.2 10.4 %collective-permute-start = (bf16[128,512]{1,0:T(8,128)(2,1)S(1)}, bf16[128,512]{1,0:T(8,128)(2,1)S(1)}, u32[]{:S(2)}, u32[]{:S(2)}) collective-permute-start(bf16[128,512]{1,0:T(8,128)(2,1)S(1)} %copy.24), channel_id=1, source_target_pairs={{0,1},{1,2},{2,3},{3,4},{4,5},{5,6},{6,7},{7,8},{8,9},{9,10},{10,1... | collective-permute-start | bytes 393224 | tf_op jit(solution)/shard_map/while/body/eval_jaxpr/ppermute | solution.py:19
  46.7 6.0 %collective-permute-start.1 = (f32[128,512]{1,0:T(8,128)}, f32[128,512]{1,0:T(8,128)S(1)}, u32[]{:S(2)}, u32[]{:S(2)}) collective-permute-start(f32[128,512]{1,0:T(8,128)} %fusion.42), channel_id=1, source_target_pairs={{0,1},{1,2},{2,3},{3,4},{4,5},{5,6},{6,7},{7,8},{8,9},{9,10},{10,1... | collective-permute-start | bytes 786440 | tf_op jit(solution)/shard_map/while/body/eval_jaxpr/ppermute | solution.py:19
  52.7 10.4 %collective-permute-start = (bf16[128,512]{1,0:T(8,128)(2,1)S(1)}, bf16[128,512]{1,0:T(8,128)(2,1)S(1)}, u32[]{:S(2)}, u32[]{:S(2)}) collective-permute-start(bf16[128,512]{1,0:T(8,128)(2,1)S(1)} %copy.24), channel_id=1, source_target_pairs={{0,1},{1,2},{2,3},{3,4},{4,5},{5,6},{6,7},{7,8},{8,9},{9,10},{10,1... | collective-permute-start | bytes 393224 | tf_op jit(solution)/shard_map/while/body/eval_jaxpr/ppermute | solution.py:19
  63.2 11.4 %collective-permute-start = (bf16[128,512]{1,0:T(8,128)(2,1)S(1)}, bf16[128,512]{1,0:T(8,128)(2,1)S(1)}, u32[]{:S(2)}, u32[]{:S(2)}) collective-permute-start(bf16[128,512]{1,0:T(8,128)(2,1)S(1)} %copy.24), channel_id=1, source_target_pairs={{0,1},{1,2},{2,3},{3,4},{4,5},{5,6},{6,7},{7,8},{8,9},{9,10},{10,1... | collective-permute-start | bytes 393224 | tf_op jit(solution)/shard_map/while/body/eval_jaxpr/ppermute | solution.py:19
  67.7 7.9 %collective-permute-start.1 = (f32[128,512]{1,0:T(8,128)}, f32[128,512]{1,0:T(8,128)S(1)}, u32[]{:S(2)}, u32[]{:S(2)}) collective-permute-start(f32[128,512]{1,0:T(8,128)} %fusion.42), channel_id=1, source_target_pairs={{0,1},{1,2},{2,3},{3,4},{4,5},{5,6},{6,7},{7,8},{8,9},{9,10},{10,1... | collective-permute-start | bytes 786440 | tf_op jit(solution)/shard_map/while/body/eval_jaxpr/ppermute | solution.py:19
  75.6 11.6 %collective-permute-start = (bf16[128,512]{1,0:T(8,128)(2,1)S(1)}, bf16[128,512]{1,0:T(8,128)(2,1)S(1)}, u32[]{:S(2)}, u32[]{:S(2)}) collective-permute-start(bf16[128,512]{1,0:T(8,128)(2,1)S(1)} %copy.24), channel_id=1, source_target_pairs={{0,1},{1,2},{2,3},{3,4},{4,5},{5,6},{6,7},{7,8},{8,9},{9,10},{10,1... | collective-permute-start | bytes 393224 | tf_op jit(solution)/shard_map/while/body/eval_jaxpr/ppermute | solution.py:19
  80.1 9.9 %collective-permute-start.1 = (f32[128,512]{1,0:T(8,128)}, f32[128,512]{1,0:T(8,128)S(1)}, u32[]{:S(2)}, u32[]{:S(2)}) collective-permute-start(f32[128,512]{1,0:T(8,128)} %fusion.42), channel_id=1, source_target_pairs={{0,1},{1,2},{2,3},{3,4},{4,5},{5,6},{6,7},{7,8},{8,9},{9,10},{10,1... | collective-permute-start | bytes 786440 | tf_op jit(solution)/shard_map/while/body/eval_jaxpr/ppermute | solution.py:19
  90.0 9.8 %collective-permute-start = (bf16[128,512]{1,0:T(8,128)(2,1)S(1)}, bf16[128,512]{1,0:T(8,128)(2,1)S(1)}, u32[]{:S(2)}, u32[]{:S(2)}) collective-permute-start(bf16[128,512]{1,0:T(8,128)(2,1)S(1)} %copy.24), channel_id=1, source_target_pairs={{0,1},{1,2},{2,3},{3,4},{4,5},{5,6},{6,7},{7,8},{8,9},{9,10},{10,1... | collective-permute-start | bytes 393224 | tf_op jit(solution)/shard_map/while/body/eval_jaxpr/ppermute | solution.py:19
  94.5 9.9 %collective-permute-start.1 = (f32[128,512]{1,0:T(8,128)}, f32[128,512]{1,0:T(8,128)S(1)}, u32[]{:S(2)}, u32[]{:S(2)}) collective-permute-start(f32[128,512]{1,0:T(8,128)} %fusion.42), channel_id=1, source_target_pairs={{0,1},{1,2},{2,3},{3,4},{4,5},{5,6},{6,7},{7,8},{8,9},{9,10},{10,1... | collective-permute-start | bytes 786440 | tf_op jit(solution)/shard_map/while/body/eval_jaxpr/ppermute | solution.py:19
  104.4 8.8 %collective-permute-start = (bf16[128,512]{1,0:T(8,128)(2,1)S(1)}, bf16[128,512]{1,0:T(8,128)(2,1)S(1)}, u32[]{:S(2)}, u32[]{:S(2)}) collective-permute-start(bf16[128,512]{1,0:T(8,128)(2,1)S(1)} %copy.24), channel_id=1, source_target_pairs={{0,1},{1,2},{2,3},{3,4},{4,5},{5,6},{6,7},{7,8},{8,9},{9,10},{10,1... | collective-permute-start | bytes 393224 | tf_op jit(solution)/shard_map/while/body/eval_jaxpr/ppermute | solution.py:19
  108.9 9.9 %collective-permute-start.1 = (f32[128,512]{1,0:T(8,128)}, f32[128,512]{1,0:T(8,128)S(1)}, u32[]{:S(2)}, u32[]{:S(2)}) collective-permute-start(f32[128,512]{1,0:T(8,128)} %fusion.42), channel_id=1, source_target_pairs={{0,1},{1,2},{2,3},{3,4},{4,5},{5,6},{6,7},{7,8},{8,9},{9,10},{10,1... | collective-permute-start | bytes 786440 | tf_op jit(solution)/shard_map/while/body/eval_jaxpr/ppermute | solution.py:19
  118.9 8.8 %collective-permute-start = (bf16[128,512]{1,0:T(8,128)(2,1)S(1)}, bf16[128,512]{1,0:T(8,128)(2,1)S(1)}, u32[]{:S(2)}, u32[]{:S(2)}) collective-permute-start(bf16[128,512]{1,0:T(8,128)(2,1)S(1)} %copy.24), channel_id=1, source_target_pairs={{0,1},{1,2},{2,3},{3,4},{4,5},{5,6},{6,7},{7,8},{8,9},{9,10},{10,1... | collective-permute-start | bytes 393224 | tf_op jit(solution)/shard_map/while/body/eval_jaxpr/ppermute | solution.py:19
  123.3 9.9 %collective-permute-start.1 = (f32[128,512]{1,0:T(8,128)}, f32[128,512]{1,0:T(8,128)S(1)}, u32[]{:S(2)}, u32[]{:S(2)}) collective-permute-start(f32[128,512]{1,0:T(8,128)} %fusion.42), channel_id=1, source_target_pairs={{0,1},{1,2},{2,3},{3,4},{4,5},{5,6},{6,7},{7,8},{8,9},{9,10},{10,1... | collective-permute-start | bytes 786440 | tf_op jit(solution)/shard_map/while/body/eval_jaxpr/ppermute | solution.py:19
  133.3 8.8 %collective-permute-start = (bf16[128,512]{1,0:T(8,128)(2,1)S(1)}, bf16[128,512]{1,0:T(8,128)(2,1)S(1)}, u32[]{:S(2)}, u32[]{:S(2)}) collective-permute-start(bf16[128,512]{1,0:T(8,128)(2,1)S(1)} %copy.24), channel_id=1, source_target_pairs={{0,1},{1,2},{2,3},{3,4},{4,5},{5,6},{6,7},{7,8},{8,9},{9,10},{10,1... | collective-permute-start | bytes 393224 | tf_op jit(solution)/shard_map/while/body/eval_jaxpr/ppermute | solution.py:19
  137.7 9.9 %collective-permute-start.1 = (f32[128,512]{1,0:T(8,128)}, f32[128,512]{1,0:T(8,128)S(1)}, u32[]{:S(2)}, u32[]{:S(2)}) collective-permute-start(f32[128,512]{1,0:T(8,128)} %fusion.42), channel_id=1, source_target_pairs={{0,1},{1,2},{2,3},{3,4},{4,5},{5,6},{6,7},{7,8},{8,9},{9,10},{10,1... | collective-permute-start | bytes 786440 | tf_op jit(solution)/shard_map/while/body/eval_jaxpr/ppermute | solution.py:19
  147.7 8.8 %collective-permute-start = (bf16[128,512]{1,0:T(8,128)(2,1)S(1)}, bf16[128,512]{1,0:T(8,128)(2,1)S(1)}, u32[]{:S(2)}, u32[]{:S(2)}) collective-permute-start(bf16[128,512]{1,0:T(8,128)(2,1)S(1)} %copy.24), channel_id=1, source_target_pairs={{0,1},{1,2},{2,3},{3,4},{4,5},{5,6},{6,7},{7,8},{8,9},{9,10},{10,1... | collective-permute-start | bytes 393224 | tf_op jit(solution)/shard_map/while/body/eval_jaxpr/ppermute | solution.py:19
  152.2 9.9 %collective-permute-start.1 = (f32[128,512]{1,0:T(8,128)}, f32[128,512]{1,0:T(8,128)S(1)}, u32[]{:S(2)}, u32[]{:S(2)}) collective-permute-start(f32[128,512]{1,0:T(8,128)} %fusion.42), channel_id=1, source_target_pairs={{0,1},{1,2},{2,3},{3,4},{4,5},{5,6},{6,7},{7,8},{8,9},{9,10},{10,1... | collective-permute-start | bytes 786440 | tf_op jit(solution)/shard_map/while/body/eval_jaxpr/ppermute | solution.py:19
  162.1 8.8 %collective-permute-start = (bf16[128,512]{1,0:T(8,128)(2,1)S(1)}, bf16[128,512]{1,0:T(8,128)(2,1)S(1)}, u32[]{:S(2)}, u32[]{:S(2)}) collective-permute-start(bf16[128,512]{1,0:T(8,128)(2,1)S(1)} %copy.24), channel_id=1, source_target_pairs={{0,1},{1,2},{2,3},{3,4},{4,5},{5,6},{6,7},{7,8},{8,9},{9,10},{10,1... | collective-permute-start | bytes 393224 | tf_op jit(solution)/shard_map/while/body/eval_jaxpr/ppermute | solution.py:19
  166.6 9.9 %collective-permute-start.1 = (f32[128,512]{1,0:T(8,128)}, f32[128,512]{1,0:T(8,128)S(1)}, u32[]{:S(2)}, u32[]{:S(2)}) collective-permute-start(f32[128,512]{1,0:T(8,128)} %fusion.42), channel_id=1, source_target_pairs={{0,1},{1,2},{2,3},{3,4},{4,5},{5,6},{6,7},{7,8},{8,9},{9,10},{10,1... | collective-permute-start | bytes 786440 | tf_op jit(solution)/shard_map/while/body/eval_jaxpr/ppermute | solution.py:19
  176.5 8.8 %collective-permute-start = (bf16[128,512]{1,0:T(8,128)(2,1)S(1)}, bf16[128,512]{1,0:T(8,128)(2,1)S(1)}, u32[]{:S(2)}, u32[]{:S(2)}) collective-permute-start(bf16[128,512]{1,0:T(8,128)(2,1)S(1)} %copy.24), channel_id=1, source_target_pairs={{0,1},{1,2},{2,3},{3,4},{4,5},{5,6},{6,7},{7,8},{8,9},{9,10},{10,1... | collective-permute-start | bytes 393224 | tf_op jit(solution)/shard_map/while/body/eval_jaxpr/ppermute | solution.py:19
  181.0 9.9 %collective-permute-start.1 = (f32[128,512]{1,0:T(8,128)}, f32[128,512]{1,0:T(8,128)S(1)}, u32[]{:S(2)}, u32[]{:S(2)}) collective-permute-start(f32[128,512]{1,0:T(8,128)} %fusion.42), channel_id=1, source_target_pairs={{0,1},{1,2},{2,3},{3,4},{4,5},{5,6},{6,7},{7,8},{8,9},{9,10},{10,1... | collective-permute-start | bytes 786440 | tf_op jit(solution)/shard_map/while/body/eval_jaxpr/ppermute | solution.py:19
  190.9 8.8 %collective-permute-start = (bf16[128,512]{1,0:T(8,128)(2,1)S(1)}, bf16[128,512]{1,0:T(8,128)(2,1)S(1)}, u32[]{:S(2)}, u32[]{:S(2)}) collective-permute-start(bf16[128,512]{1,0:T(8,128)(2,1)S(1)} %copy.24), channel_id=1, source_target_pairs={{0,1},{1,2},{2,3},{3,4},{4,5},{5,6},{6,7},{7,8},{8,9},{9,10},{10,1... | collective-permute-start | bytes 393224 | tf_op jit(solution)/shard_map/while/body/eval_jaxpr/ppermute | solution.py:19
  195.4 9.9 %collective-permute-start.1 = (f32[128,512]{1,0:T(8,128)}, f32[128,512]{1,0:T(8,128)S(1)}, u32[]{:S(2)}, u32[]{:S(2)}) collective-permute-start(f32[128,512]{1,0:T(8,128)} %fusion.42), channel_id=1, source_target_pairs={{0,1},{1,2},{2,3},{3,4},{4,5},{5,6},{6,7},{7,8},{8,9},{9,10},{10,1... | collective-permute-start | bytes 786440 | tf_op jit(solution)/shard_map/while/body/eval_jaxpr/ppermute | solution.py:19
  205.3 8.8 %collective-permute-start = (bf16[128,512]{1,0:T(8,128)(2,1)S(1)}, bf16[128,512]{1,0:T(8,128)(2,1)S(1)}, u32[]{:S(2)}, u32[]{:S(2)}) collective-permute-start(bf16[128,512]{1,0:T(8,128)(2,1)S(1)} %copy.24), channel_id=1, source_target_pairs={{0,1},{1,2},{2,3},{3,4},{4,5},{5,6},{6,7},{7,8},{8,9},{9,10},{10,1... | collective-permute-start | bytes 393224 | tf_op jit(solution)/shard_map/while/body/eval_jaxpr/ppermute | solution.py:19
  209.8 9.9 %collective-permute-start.1 = (f32[128,512]{1,0:T(8,128)}, f32[128,512]{1,0:T(8,128)S(1)}, u32[]{:S(2)}, u32[]{:S(2)}) collective-permute-start(f32[128,512]{1,0:T(8,128)} %fusion.42), channel_id=1, source_target_pairs={{0,1},{1,2},{2,3},{3,4},{4,5},{5,6},{6,7},{7,8},{8,9},{9,10},{10,1... | collective-permute-start | bytes 786440 | tf_op jit(solution)/shard_map/while/body/eval_jaxpr/ppermute | solution.py:19
  219.7 8.8 %collective-permute-start = (bf16[128,512]{1,0:T(8,128)(2,1)S(1)}, bf16[128,512]{1,0:T(8,128)(2,1)S(1)}, u32[]{:S(2)}, u32[]{:S(2)}) collective-permute-start(bf16[128,512]{1,0:T(8,128)(2,1)S(1)} %copy.24), channel_id=1, source_target_pairs={{0,1},{1,2},{2,3},{3,4},{4,5},{5,6},{6,7},{7,8},{8,9},{9,10},{10,1... | collective-permute-start | bytes 393224 | tf_op jit(solution)/shard_map/while/body/eval_jaxpr/ppermute | solution.py:19
  224.2 9.9 %collective-permute-start.1 = (f32[128,512]{1,0:T(8,128)}, f32[128,512]{1,0:T(8,128)S(1)}, u32[]{:S(2)}, u32[]{:S(2)}) collective-permute-start(f32[128,512]{1,0:T(8,128)} %fusion.42), channel_id=1, source_target_pairs={{0,1},{1,2},{2,3},{3,4},{4,5},{5,6},{6,7},{7,8},{8,9},{9,10},{10,1... | collective-permute-start | bytes 786440 | tf_op jit(solution)/shard_map/while/body/eval_jaxpr/ppermute | solution.py:19
  234.2 8.8 %collective-permute-start = (bf16[128,512]{1,0:T(8,128)(2,1)S(1)}, bf16[128,512]{1,0:T(8,128)(2,1)S(1)}, u32[]{:S(2)}, u32[]{:S(2)}) collective-permute-start(bf16[128,512]{1,0:T(8,128)(2,1)S(1)} %copy.24), channel_id=1, source_target_pairs={{0,1},{1,2},{2,3},{3,4},{4,5},{5,6},{6,7},{7,8},{8,9},{9,10},{10,1... | collective-permute-start | bytes 393224 | tf_op jit(solution)/shard_map/while/body/eval_jaxpr/ppermute | solution.py:19
  238.6 9.9 %collective-permute-start.1 = (f32[128,512]{1,0:T(8,128)}, f32[128,512]{1,0:T(8,128)S(1)}, u32[]{:S(2)}, u32[]{:S(2)}) collective-permute-start(f32[128,512]{1,0:T(8,128)} %fusion.42), channel_id=1, source_target_pairs={{0,1},{1,2},{2,3},{3,4},{4,5},{5,6},{6,7},{7,8},{8,9},{9,10},{10,1... | collective-permute-start | bytes 786440 | tf_op jit(solution)/shard_map/while/body/eval_jaxpr/ppermute | solution.py:19
  248.6 8.8 %collective-permute-start = (bf16[128,512]{1,0:T(8,128)(2,1)S(1)}, bf16[128,512]{1,0:T(8,128)(2,1)S(1)}, u32[]{:S(2)}, u32[]{:S(2)}) collective-permute-start(bf16[128,512]{1,0:T(8,128)(2,1)S(1)} %copy.24), channel_id=1, source_target_pairs={{0,1},{1,2},{2,3},{3,4},{4,5},{5,6},{6,7},{7,8},{8,9},{9,10},{10,1... | collective-permute-start | bytes 393224 | tf_op jit(solution)/shard_map/while/body/eval_jaxpr/ppermute | solution.py:19
  253.0 9.9 %collective-permute-start.1 = (f32[128,512]{1,0:T(8,128)}, f32[128,512]{1,0:T(8,128)S(1)}, u32[]{:S(2)}, u32[]{:S(2)}) collective-permute-start(f32[128,512]{1,0:T(8,128)} %fusion.42), channel_id=1, source_target_pairs={{0,1},{1,2},{2,3},{3,4},{4,5},{5,6},{6,7},{7,8},{8,9},{9,10},{10,1... | collective-permute-start | bytes 786440 | tf_op jit(solution)/shard_map/while/body/eval_jaxpr/ppermute | solution.py:19
  263.0 8.8 %collective-permute-start = (bf16[128,512]{1,0:T(8,128)(2,1)S(1)}, bf16[128,512]{1,0:T(8,128)(2,1)S(1)}, u32[]{:S(2)}, u32[]{:S(2)}) collective-permute-start(bf16[128,512]{1,0:T(8,128)(2,1)S(1)} %copy.24), channel_id=1, source_target_pairs={{0,1},{1,2},{2,3},{3,4},{4,5},{5,6},{6,7},{7,8},{8,9},{9,10},{10,1... | collective-permute-start | bytes 393224 | tf_op jit(solution)/shard_map/while/body/eval_jaxpr/ppermute | solution.py:19
  267.5 9.9 %collective-permute-start.1 = (f32[128,512]{1,0:T(8,128)}, f32[128,512]{1,0:T(8,128)S(1)}, u32[]{:S(2)}, u32[]{:S(2)}) collective-permute-start(f32[128,512]{1,0:T(8,128)} %fusion.42), channel_id=1, source_target_pairs={{0,1},{1,2},{2,3},{3,4},{4,5},{5,6},{6,7},{7,8},{8,9},{9,10},{10,1... | collective-permute-start | bytes 786440 | tf_op jit(solution)/shard_map/while/body/eval_jaxpr/ppermute | solution.py:19
  277.4 8.8 %collective-permute-start = (bf16[128,512]{1,0:T(8,128)(2,1)S(1)}, bf16[128,512]{1,0:T(8,128)(2,1)S(1)}, u32[]{:S(2)}, u32[]{:S(2)}) collective-permute-start(bf16[128,512]{1,0:T(8,128)(2,1)S(1)} %copy.24), channel_id=1, source_target_pairs={{0,1},{1,2},{2,3},{3,4},{4,5},{5,6},{6,7},{7,8},{8,9},{9,10},{10,1... | collective-permute-start | bytes 393224 | tf_op jit(solution)/shard_map/while/body/eval_jaxpr/ppermute | solution.py:19
  281.9 9.9 %collective-permute-start.1 = (f32[128,512]{1,0:T(8,128)}, f32[128,512]{1,0:T(8,128)S(1)}, u32[]{:S(2)}, u32[]{:S(2)}) collective-permute-start(f32[128,512]{1,0:T(8,128)} %fusion.42), channel_id=1, source_target_pairs={{0,1},{1,2},{2,3},{3,4},{4,5},{5,6},{6,7},{7,8},{8,9},{9,10},{10,1... | collective-permute-start | bytes 786440 | tf_op jit(solution)/shard_map/while/body/eval_jaxpr/ppermute | solution.py:19
  291.8 8.8 %collective-permute-start = (bf16[128,512]{1,0:T(8,128)(2,1)S(1)}, bf16[128,512]{1,0:T(8,128)(2,1)S(1)}, u32[]{:S(2)}, u32[]{:S(2)}) collective-permute-start(bf16[128,512]{1,0:T(8,128)(2,1)S(1)} %copy.24), channel_id=1, source_target_pairs={{0,1},{1,2},{2,3},{3,4},{4,5},{5,6},{6,7},{7,8},{8,9},{9,10},{10,1... | collective-permute-start | bytes 393224 | tf_op jit(solution)/shard_map/while/body/eval_jaxpr/ppermute | solution.py:19
  296.3 9.9 %collective-permute-start.1 = (f32[128,512]{1,0:T(8,128)}, f32[128,512]{1,0:T(8,128)S(1)}, u32[]{:S(2)}, u32[]{:S(2)}) collective-permute-start(f32[128,512]{1,0:T(8,128)} %fusion.42), channel_id=1, source_target_pairs={{0,1},{1,2},{2,3},{3,4},{4,5},{5,6},{6,7},{7,8},{8,9},{9,10},{10,1... | collective-permute-start | bytes 786440 | tf_op jit(solution)/shard_map/while/body/eval_jaxpr/ppermute | solution.py:19
  306.2 8.8 %collective-permute-start = (bf16[128,512]{1,0:T(8,128)(2,1)S(1)}, bf16[128,512]{1,0:T(8,128)(2,1)S(1)}, u32[]{:S(2)}, u32[]{:S(2)}) collective-permute-start(bf16[128,512]{1,0:T(8,128)(2,1)S(1)} %copy.24), channel_id=1, source_target_pairs={{0,1},{1,2},{2,3},{3,4},{4,5},{5,6},{6,7},{7,8},{8,9},{9,10},{10,1... | collective-permute-start | bytes 393224 | tf_op jit(solution)/shard_map/while/body/eval_jaxpr/ppermute | solution.py:19
  310.7 9.9 %collective-permute-start.1 = (f32[128,512]{1,0:T(8,128)}, f32[128,512]{1,0:T(8,128)S(1)}, u32[]{:S(2)}, u32[]{:S(2)}) collective-permute-start(f32[128,512]{1,0:T(8,128)} %fusion.42), channel_id=1, source_target_pairs={{0,1},{1,2},{2,3},{3,4},{4,5},{5,6},{6,7},{7,8},{8,9},{9,10},{10,1... | collective-permute-start | bytes 786440 | tf_op jit(solution)/shard_map/while/body/eval_jaxpr/ppermute | solution.py:19
  320.6 8.8 %collective-permute-start = (bf16[128,512]{1,0:T(8,128)(2,1)S(1)}, bf16[128,512]{1,0:T(8,128)(2,1)S(1)}, u32[]{:S(2)}, u32[]{:S(2)}) collective-permute-start(bf16[128,512]{1,0:T(8,128)(2,1)S(1)} %copy.24), channel_id=1, source_target_pairs={{0,1},{1,2},{2,3},{3,4},{4,5},{5,6},{6,7},{7,8},{8,9},{9,10},{10,1... | collective-permute-start | bytes 393224 | tf_op jit(solution)/shard_map/while/body/eval_jaxpr/ppermute | solution.py:19
  325.1 9.9 %collective-permute-start.1 = (f32[128,512]{1,0:T(8,128)}, f32[128,512]{1,0:T(8,128)S(1)}, u32[]{:S(2)}, u32[]{:S(2)}) collective-permute-start(f32[128,512]{1,0:T(8,128)} %fusion.42), channel_id=1, source_target_pairs={{0,1},{1,2},{2,3},{3,4},{4,5},{5,6},{6,7},{7,8},{8,9},{9,10},{10,1... | collective-permute-start | bytes 786440 | tf_op jit(solution)/shard_map/while/body/eval_jaxpr/ppermute | solution.py:19
  335.0 8.8 %collective-permute-start = (bf16[128,512]{1,0:T(8,128)(2,1)S(1)}, bf16[128,512]{1,0:T(8,128)(2,1)S(1)}, u32[]{:S(2)}, u32[]{:S(2)}) collective-permute-start(bf16[128,512]{1,0:T(8,128)(2,1)S(1)} %copy.24), channel_id=1, source_target_pairs={{0,1},{1,2},{2,3},{3,4},{4,5},{5,6},{6,7},{7,8},{8,9},{9,10},{10,1... | collective-permute-start | bytes 393224 | tf_op jit(solution)/shard_map/while/body/eval_jaxpr/ppermute | solution.py:19
  339.5 9.9 %collective-permute-start.1 = (f32[128,512]{1,0:T(8,128)}, f32[128,512]{1,0:T(8,128)S(1)}, u32[]{:S(2)}, u32[]{:S(2)}) collective-permute-start(f32[128,512]{1,0:T(8,128)} %fusion.42), channel_id=1, source_target_pairs={{0,1},{1,2},{2,3},{3,4},{4,5},{5,6},{6,7},{7,8},{8,9},{9,10},{10,1... | collective-permute-start | bytes 786440 | tf_op jit(solution)/shard_map/while/body/eval_jaxpr/ppermute | solution.py:19
  349.5 8.8 %collective-permute-start = (bf16[128,512]{1,0:T(8,128)(2,1)S(1)}, bf16[128,512]{1,0:T(8,128)(2,1)S(1)}, u32[]{:S(2)}, u32[]{:S(2)}) collective-permute-start(bf16[128,512]{1,0:T(8,128)(2,1)S(1)} %copy.24), channel_id=1, source_target_pairs={{0,1},{1,2},{2,3},{3,4},{4,5},{5,6},{6,7},{7,8},{8,9},{9,10},{10,1... | collective-permute-start | bytes 393224 | tf_op jit(solution)/shard_map/while/body/eval_jaxpr/ppermute | solution.py:19
  353.9 9.9 %collective-permute-start.1 = (f32[128,512]{1,0:T(8,128)}, f32[128,512]{1,0:T(8,128)S(1)}, u32[]{:S(2)}, u32[]{:S(2)}) collective-permute-start(f32[128,512]{1,0:T(8,128)} %fusion.42), channel_id=1, source_target_pairs={{0,1},{1,2},{2,3},{3,4},{4,5},{5,6},{6,7},{7,8},{8,9},{9,10},{10,1... | collective-permute-start | bytes 786440 | tf_op jit(solution)/shard_map/while/body/eval_jaxpr/ppermute | solution.py:19
  363.9 8.8 %collective-permute-start = (bf16[128,512]{1,0:T(8,128)(2,1)S(1)}, bf16[128,512]{1,0:T(8,128)(2,1)S(1)}, u32[]{:S(2)}, u32[]{:S(2)}) collective-permute-start(bf16[128,512]{1,0:T(8,128)(2,1)S(1)} %copy.24), channel_id=1, source_target_pairs={{0,1},{1,2},{2,3},{3,4},{4,5},{5,6},{6,7},{7,8},{8,9},{9,10},{10,1... | collective-permute-start | bytes 393224 | tf_op jit(solution)/shard_map/while/body/eval_jaxpr/ppermute | solution.py:19
  368.3 9.9 %collective-permute-start.1 = (f32[128,512]{1,0:T(8,128)}, f32[128,512]{1,0:T(8,128)S(1)}, u32[]{:S(2)}, u32[]{:S(2)}) collective-permute-start(f32[128,512]{1,0:T(8,128)} %fusion.42), channel_id=1, source_target_pairs={{0,1},{1,2},{2,3},{3,4},{4,5},{5,6},{6,7},{7,8},{8,9},{9,10},{10,1... | collective-permute-start | bytes 786440 | tf_op jit(solution)/shard_map/while/body/eval_jaxpr/ppermute | solution.py:19
  378.3 8.8 %collective-permute-start = (bf16[128,512]{1,0:T(8,128)(2,1)S(1)}, bf16[128,512]{1,0:T(8,128)(2,1)S(1)}, u32[]{:S(2)}, u32[]{:S(2)}) collective-permute-start(bf16[128,512]{1,0:T(8,128)(2,1)S(1)} %copy.24), channel_id=1, source_target_pairs={{0,1},{1,2},{2,3},{3,4},{4,5},{5,6},{6,7},{7,8},{8,9},{9,10},{10,1... | collective-permute-start | bytes 393224 | tf_op jit(solution)/shard_map/while/body/eval_jaxpr/ppermute | solution.py:19
  382.8 9.9 %collective-permute-start.1 = (f32[128,512]{1,0:T(8,128)}, f32[128,512]{1,0:T(8,128)S(1)}, u32[]{:S(2)}, u32[]{:S(2)}) collective-permute-start(f32[128,512]{1,0:T(8,128)} %fusion.42), channel_id=1, source_target_pairs={{0,1},{1,2},{2,3},{3,4},{4,5},{5,6},{6,7},{7,8},{8,9},{9,10},{10,1... | collective-permute-start | bytes 786440 | tf_op jit(solution)/shard_map/while/body/eval_jaxpr/ppermute | solution.py:19
  392.7 8.8 %collective-permute-start = (bf16[128,512]{1,0:T(8,128)(2,1)S(1)}, bf16[128,512]{1,0:T(8,128)(2,1)S(1)}, u32[]{:S(2)}, u32[]{:S(2)}) collective-permute-start(bf16[128,512]{1,0:T(8,128)(2,1)S(1)} %copy.24), channel_id=1, source_target_pairs={{0,1},{1,2},{2,3},{3,4},{4,5},{5,6},{6,7},{7,8},{8,9},{9,10},{10,1... | collective-permute-start | bytes 393224 | tf_op jit(solution)/shard_map/while/body/eval_jaxpr/ppermute | solution.py:19
  397.2 9.9 %collective-permute-start.1 = (f32[128,512]{1,0:T(8,128)}, f32[128,512]{1,0:T(8,128)S(1)}, u32[]{:S(2)}, u32[]{:S(2)}) collective-permute-start(f32[128,512]{1,0:T(8,128)} %fusion.42), channel_id=1, source_target_pairs={{0,1},{1,2},{2,3},{3,4},{4,5},{5,6},{6,7},{7,8},{8,9},{9,10},{10,1... | collective-permute-start | bytes 786440 | tf_op jit(solution)/shard_map/while/body/eval_jaxpr/ppermute | solution.py:19
  407.1 8.8 %collective-permute-start = (bf16[128,512]{1,0:T(8,128)(2,1)S(1)}, bf16[128,512]{1,0:T(8,128)(2,1)S(1)}, u32[]{:S(2)}, u32[]{:S(2)}) collective-permute-start(bf16[128,512]{1,0:T(8,128)(2,1)S(1)} %copy.24), channel_id=1, source_target_pairs={{0,1},{1,2},{2,3},{3,4},{4,5},{5,6},{6,7},{7,8},{8,9},{9,10},{10,1... | collective-permute-start | bytes 393224 | tf_op jit(solution)/shard_map/while/body/eval_jaxpr/ppermute | solution.py:19
  411.6 9.9 %collective-permute-start.1 = (f32[128,512]{1,0:T(8,128)}, f32[128,512]{1,0:T(8,128)S(1)}, u32[]{:S(2)}, u32[]{:S(2)}) collective-permute-start(f32[128,512]{1,0:T(8,128)} %fusion.42), channel_id=1, source_target_pairs={{0,1},{1,2},{2,3},{3,4},{4,5},{5,6},{6,7},{7,8},{8,9},{9,10},{10,1... | collective-permute-start | bytes 786440 | tf_op jit(solution)/shard_map/while/body/eval_jaxpr/ppermute | solution.py:19
  421.5 8.8 %collective-permute-start = (bf16[128,512]{1,0:T(8,128)(2,1)S(1)}, bf16[128,512]{1,0:T(8,128)(2,1)S(1)}, u32[]{:S(2)}, u32[]{:S(2)}) collective-permute-start(bf16[128,512]{1,0:T(8,128)(2,1)S(1)} %copy.24), channel_id=1, source_target_pairs={{0,1},{1,2},{2,3},{3,4},{4,5},{5,6},{6,7},{7,8},{8,9},{9,10},{10,1... | collective-permute-start | bytes 393224 | tf_op jit(solution)/shard_map/while/body/eval_jaxpr/ppermute | solution.py:19
  426.0 9.9 %collective-permute-start.1 = (f32[128,512]{1,0:T(8,128)}, f32[128,512]{1,0:T(8,128)S(1)}, u32[]{:S(2)}, u32[]{:S(2)}) collective-permute-start(f32[128,512]{1,0:T(8,128)} %fusion.42), channel_id=1, source_target_pairs={{0,1},{1,2},{2,3},{3,4},{4,5},{5,6},{6,7},{7,8},{8,9},{9,10},{10,1... | collective-permute-start | bytes 786440 | tf_op jit(solution)/shard_map/while/body/eval_jaxpr/ppermute | solution.py:19
  435.9 8.8 %collective-permute-start = (bf16[128,512]{1,0:T(8,128)(2,1)S(1)}, bf16[128,512]{1,0:T(8,128)(2,1)S(1)}, u32[]{:S(2)}, u32[]{:S(2)}) collective-permute-start(bf16[128,512]{1,0:T(8,128)(2,1)S(1)} %copy.24), channel_id=1, source_target_pairs={{0,1},{1,2},{2,3},{3,4},{4,5},{5,6},{6,7},{7,8},{8,9},{9,10},{10,1... | collective-permute-start | bytes 393224 | tf_op jit(solution)/shard_map/while/body/eval_jaxpr/ppermute | solution.py:19
  440.4 9.9 %collective-permute-start.1 = (f32[128,512]{1,0:T(8,128)}, f32[128,512]{1,0:T(8,128)S(1)}, u32[]{:S(2)}, u32[]{:S(2)}) collective-permute-start(f32[128,512]{1,0:T(8,128)} %fusion.42), channel_id=1, source_target_pairs={{0,1},{1,2},{2,3},{3,4},{4,5},{5,6},{6,7},{7,8},{8,9},{9,10},{10,1... | collective-permute-start | bytes 786440 | tf_op jit(solution)/shard_map/while/body/eval_jaxpr/ppermute | solution.py:19
  450.3 8.8 %collective-permute-start = (bf16[128,512]{1,0:T(8,128)(2,1)S(1)}, bf16[128,512]{1,0:T(8,128)(2,1)S(1)}, u32[]{:S(2)}, u32[]{:S(2)}) collective-permute-start(bf16[128,512]{1,0:T(8,128)(2,1)S(1)} %copy.24), channel_id=1, source_target_pairs={{0,1},{1,2},{2,3},{3,4},{4,5},{5,6},{6,7},{7,8},{8,9},{9,10},{10,1... | collective-permute-start | bytes 393224 | tf_op jit(solution)/shard_map/while/body/eval_jaxpr/ppermute | solution.py:19
  454.8 9.9 %collective-permute-start.1 = (f32[128,512]{1,0:T(8,128)}, f32[128,512]{1,0:T(8,128)S(1)}, u32[]{:S(2)}, u32[]{:S(2)}) collective-permute-start(f32[128,512]{1,0:T(8,128)} %fusion.42), channel_id=1, source_target_pairs={{0,1},{1,2},{2,3},{3,4},{4,5},{5,6},{6,7},{7,8},{8,9},{9,10},{10,1... | collective-permute-start | bytes 786440 | tf_op jit(solution)/shard_map/while/body/eval_jaxpr/ppermute | solution.py:19
  467.1 9.7 %collective-permute-start.2 = (f32[128,512]{1,0:T(8,128)S(1)}, f32[128,512]{1,0:T(8,128)S(1)}, u32[]{:S(2)}, u32[]{:S(2)}) collective-permute-start(f32[128,512]{1,0:T(8,128)S(1)} %fusion.15), channel_id=1, source_target_pairs={{0,1},{1,2},{2,3},{3,4},{4,5},{5,6},{6,7},{7,8},{8,9},{9,10},{10,1... | collective-permute-start | bytes 786440 | tf_op jit(solution)/shard_map/ppermute | solution.py:19
  (8 other events, 155.3 us)
Sparse Core Ops, SparseCore 0:
  477.6 91.5 reduce-scatter.1
